TPU v7x, 256 devices: a whole 4x4x8 slice. The times are simulated.
256 devices in a mesh: vgrp: 4 (over y), samp: 64 (over z, x, core).
Axes of the slice: x: 4, y: 4, z: 8, core: 2. Of those that a mesh axis runs over, the one named last changes fastest.
Arguments:
- phenotype: float32 [196608], P(('vgrp', 'samp')), may hold values from -6 to 6
- exposures: float32 [196608, 128], P('samp'), may hold values from -6 to 6
- perms: int32 [16, 196608], P(None, 'samp'), may hold values from 0 to 196607, each once within a row
- genotypes: int32 [196608, 2048], P('samp', 'vgrp'), may hold values from 0 to 2
Outputs:
- statistics: float32 [2048, 16], P(('vgrp', 'samp'))
Inputs may be any that keep to these rules, and one draw needn't show every extreme that they name: Each row of perms holds every sample index once.
All inputs are finite; a program needn't handle non-finite values.
Results may differ from a plain program's by a relative error of at most 0.00075.
Values sent between devices are 32-bit elements; how exact they have to be, the bound alone decides.
No kernel may reach another device: no remote copies, remote signals or barrier semaphores. Data moves between devices by JAX's collectives and lax.ppermute only.
A program may use at most 64 MiB of HBM per device.

v0:
```python
import jax
import jax.numpy as jnp
from jax import lax
from jax.sharding import PartitionSpec as P


def chol_solve(factor, rhs):
    middle = lax.linalg.triangular_solve(factor, rhs, left_side=True, lower=True)
    return lax.linalg.triangular_solve(factor, middle, left_side=True, lower=True, transpose_a=True)


def permute_rows(pheno_full, perms):
    samples = pheno_full.shape[0]
    table = pheno_full.reshape(samples // 128, 128)
    lanes = lax.broadcasted_iota(jnp.int32, (1, 128), 1)

    def one_perm(index_row):
        picked_rows = table[index_row // 128]
        wanted = (index_row % 128)[:, None] == lanes
        return jnp.sum(jnp.where(wanted, picked_rows, jnp.float32(0.0)), axis=1)

    return lax.map(one_perm, perms)


def per_device(phenotype, exposures, perms, genotypes):
    hi = lax.Precision.HIGHEST
    pheno_full = lax.all_gather(phenotype, ("vgrp", "samp"), axis=0, tiled=True)
    samples = pheno_full.shape[0]
    local_rows = exposures.shape[0]
    width = exposures.shape[1]
    quarter = local_rows // lax.axis_size("vgrp")
    offset_rows = lax.axis_index("vgrp") * quarter
    perm_rows = permute_rows(pheno_full, perms)
    expo_part = lax.dynamic_slice_in_dim(exposures, offset_rows, quarter, 0)
    pheno_part = lax.dynamic_slice_in_dim(perm_rows, offset_rows, quarter, 1)
    gram_part = jnp.dot(expo_part.T, expo_part, precision=hi)
    cross_part = jnp.dot(expo_part.T, pheno_part.T, precision=hi)
    gram, cross = lax.psum((gram_part, cross_part), ("vgrp", "samp"))
    system = gram + 0.5 * samples * jnp.eye(width, dtype=jnp.float32)
    factor = jnp.linalg.cholesky(system)
    coefficients = chol_solve(factor, cross)
    permuted = jnp.transpose(perm_rows)
    residuals = permuted - jnp.dot(exposures, coefficients, precision=hi)
    nperm = residuals.shape[1]
    weighted = (
        (exposures[:, :, None] * residuals[:, None, :])
        .reshape(local_rows, width * nperm)
        .astype(jnp.bfloat16)
    )
    dosages = genotypes.astype(jnp.bfloat16)
    own_rows = genotypes.shape[1] // lax.axis_size("samp")
    summed = lax.psum(jnp.dot(dosages.T, weighted, preferred_element_type=jnp.float32), "samp")
    own_scores = lax.dynamic_slice_in_dim(summed, lax.axis_index("samp") * own_rows, own_rows, 0)
    shaped = own_scores.reshape(own_rows, width, nperm)
    return jnp.sum(shaped * shaped, axis=1) / (samples * width)


def solution(mesh):
    return jax.shard_map(
        per_device,
        mesh=mesh,
        in_specs=(P(("vgrp", "samp")), P("samp", None), P(None, "samp"), P("samp", "vgrp")),
        out_specs=P(("vgrp", "samp"), None),
        check_vma=False,
    )
```

profile of v0, /device:TPU:8, one launch (start us, length us, event | category | flops | bytes accessed | tf_op | source)
XLA Modules:
  0.0 587.2 jit_solution(16091386227517214379)
XLA Ops:
  6.5 2.6 fusion.7
  9.9 77.2 %all-gather = f32[256,1,768]{2,1,0:T(1,128)S(1)} all-gather(f32[1,1,768]{2,1,0:T(1,128)S(1)} %reshape.133), channel_id=1, replica_groups=mesh['vgrp'=4,'samp'=64] {'vgrp','samp'}, dimensions={0}, use_global_device_ids=true | all-gather | bytes 789504 | tf_op jit(solution)/shard_map/all_gather | solution.py:27
  87.0 181.6 %while.13 = (s32[]{:T(128)}, f32[16,3072]{1,0:T(8,128)S(1)}, s32[16,3072]{1,0:T(8,128)}, f32[1536,128]{1,0:T(8,128)S(1)}, s32[]{:T(128)}, /*index=5*/s32[]{:T(128)}) while((s32[]{:T(128)}, f32[16,3072]{1,0:T(8,128)S(1)}, s32[16,3072]{1,0:T(8,128)}, f32[1536,128]{1,0:T(8,128)S(1)}, s32[]{:T(128)}, /*index=5*/s32[]{:T(128)}) %tuple.39), condition=%wide.region_2.3_spmd.clone, body=%wide.region_0.2_spmd.clone.sunk | while | flops 1268738 | bytes 4866133 | solution.py:22
  88.0 8.1 %gather_fusion = f32[3072,128]{1,0:T(8,128)S(1)} fusion(f32[1536,128]{1,0:T(8,128)S(1)} %get-tuple-element.138, s32[3072]{0:T(1024)S(1)} %broadcast_clamp_fusion.2), kind=kCustom, calls=%fused_computation.clone.clone.1 | custom fusion | bytes 3158016 | tf_op jit(solution)/shard_map/while/body/eval_jaxpr/gather | solution.py:18
  96.2 1.9 select_reduce_fusion.3
  99.4 8.1 %gather_fusion = f32[3072,128]{1,0:T(8,128)S(1)} fusion(f32[1536,128]{1,0:T(8,128)S(1)} %get-tuple-element.138, s32[3072]{0:T(1024)S(1)} %broadcast_clamp_fusion.2), kind=kCustom, calls=%fused_computation.clone.clone.1 | custom fusion | bytes 3158016 | tf_op jit(solution)/shard_map/while/body/eval_jaxpr/gather | solution.py:18
  107.5 1.9 select_reduce_fusion.3
  110.7 8.1 %gather_fusion = f32[3072,128]{1,0:T(8,128)S(1)} fusion(f32[1536,128]{1,0:T(8,128)S(1)} %get-tuple-element.138, s32[3072]{0:T(1024)S(1)} %broadcast_clamp_fusion.2), kind=kCustom, calls=%fused_computation.clone.clone.1 | custom fusion | bytes 3158016 | tf_op jit(solution)/shard_map/while/body/eval_jaxpr/gather | solution.py:18
  122.1 8.1 %gather_fusion = f32[3072,128]{1,0:T(8,128)S(1)} fusion(f32[1536,128]{1,0:T(8,128)S(1)} %get-tuple-element.138, s32[3072]{0:T(1024)S(1)} %broadcast_clamp_fusion.2), kind=kCustom, calls=%fused_computation.clone.clone.1 | custom fusion | bytes 3158016 | tf_op jit(solution)/shard_map/while/body/eval_jaxpr/gather | solution.py:18
  133.4 8.1 %gather_fusion = f32[3072,128]{1,0:T(8,128)S(1)} fusion(f32[1536,128]{1,0:T(8,128)S(1)} %get-tuple-element.138, s32[3072]{0:T(1024)S(1)} %broadcast_clamp_fusion.2), kind=kCustom, calls=%fused_computation.clone.clone.1 | custom fusion | bytes 3158016 | tf_op jit(solution)/shard_map/while/body/eval_jaxpr/gather | solution.py:18
  141.6 1.9 select_reduce_fusion.3
  144.8 8.1 %gather_fusion = f32[3072,128]{1,0:T(8,128)S(1)} fusion(f32[1536,128]{1,0:T(8,128)S(1)} %get-tuple-element.138, s32[3072]{0:T(1024)S(1)} %broadcast_clamp_fusion.2), kind=kCustom, calls=%fused_computation.clone.clone.1 | custom fusion | bytes 3158016 | tf_op jit(solution)/shard_map/while/body/eval_jaxpr/gather | solution.py:18
  156.1 8.1 %gather_fusion = f32[3072,128]{1,0:T(8,128)S(1)} fusion(f32[1536,128]{1,0:T(8,128)S(1)} %get-tuple-element.138, s32[3072]{0:T(1024)S(1)} %broadcast_clamp_fusion.2), kind=kCustom, calls=%fused_computation.clone.clone.1 | custom fusion | bytes 3158016 | tf_op jit(solution)/shard_map/while/body/eval_jaxpr/gather | solution.py:18
  167.5 8.1 %gather_fusion = f32[3072,128]{1,0:T(8,128)S(1)} fusion(f32[1536,128]{1,0:T(8,128)S(1)} %get-tuple-element.138, s32[3072]{0:T(1024)S(1)} %broadcast_clamp_fusion.2), kind=kCustom, calls=%fused_computation.clone.clone.1 | custom fusion | bytes 3158016 | tf_op jit(solution)/shard_map/while/body/eval_jaxpr/gather | solution.py:18
  175.6 1.9 select_reduce_fusion.3
  178.8 8.1 %gather_fusion = f32[3072,128]{1,0:T(8,128)S(1)} fusion(f32[1536,128]{1,0:T(8,128)S(1)} %get-tuple-element.138, s32[3072]{0:T(1024)S(1)} %broadcast_clamp_fusion.2), kind=kCustom, calls=%fused_computation.clone.clone.1 | custom fusion | bytes 3158016 | tf_op jit(solution)/shard_map/while/body/eval_jaxpr/gather | solution.py:18
  187.0 1.9 select_reduce_fusion.3
  190.2 8.1 %gather_fusion = f32[3072,128]{1,0:T(8,128)S(1)} fusion(f32[1536,128]{1,0:T(8,128)S(1)} %get-tuple-element.138, s32[3072]{0:T(1024)S(1)} %broadcast_clamp_fusion.2), kind=kCustom, calls=%fused_computation.clone.clone.1 | custom fusion | bytes 3158016 | tf_op jit(solution)/shard_map/while/body/eval_jaxpr/gather | solution.py:18
  198.3 1.9 select_reduce_fusion.3
  201.6 8.1 %gather_fusion = f32[3072,128]{1,0:T(8,128)S(1)} fusion(f32[1536,128]{1,0:T(8,128)S(1)} %get-tuple-element.138, s32[3072]{0:T(1024)S(1)} %broadcast_clamp_fusion.2), kind=kCustom, calls=%fused_computation.clone.clone.1 | custom fusion | bytes 3158016 | tf_op jit(solution)/shard_map/while/body/eval_jaxpr/gather | solution.py:18
  212.9 8.1 %gather_fusion = f32[3072,128]{1,0:T(8,128)S(1)} fusion(f32[1536,128]{1,0:T(8,128)S(1)} %get-tuple-element.138, s32[3072]{0:T(1024)S(1)} %broadcast_clamp_fusion.2), kind=kCustom, calls=%fused_computation.clone.clone.1 | custom fusion | bytes 3158016 | tf_op jit(solution)/shard_map/while/body/eval_jaxpr/gather | solution.py:18
  224.3 8.1 %gather_fusion = f32[3072,128]{1,0:T(8,128)S(1)} fusion(f32[1536,128]{1,0:T(8,128)S(1)} %get-tuple-element.138, s32[3072]{0:T(1024)S(1)} %broadcast_clamp_fusion.2), kind=kCustom, calls=%fused_computation.clone.clone.1 | custom fusion | bytes 3158016 | tf_op jit(solution)/shard_map/while/body/eval_jaxpr/gather | solution.py:18
  235.6 8.1 %gather_fusion = f32[3072,128]{1,0:T(8,128)S(1)} fusion(f32[1536,128]{1,0:T(8,128)S(1)} %get-tuple-element.138, s32[3072]{0:T(1024)S(1)} %broadcast_clamp_fusion.2), kind=kCustom, calls=%fused_computation.clone.clone.1 | custom fusion | bytes 3158016 | tf_op jit(solution)/shard_map/while/body/eval_jaxpr/gather | solution.py:18
  247.0 8.1 %gather_fusion = f32[3072,128]{1,0:T(8,128)S(1)} fusion(f32[1536,128]{1,0:T(8,128)S(1)} %get-tuple-element.138, s32[3072]{0:T(1024)S(1)} %broadcast_clamp_fusion.2), kind=kCustom, calls=%fused_computation.clone.clone.1 | custom fusion | bytes 3158016 | tf_op jit(solution)/shard_map/while/body/eval_jaxpr/gather | solution.py:18
  258.3 8.1 %gather_fusion = f32[3072,128]{1,0:T(8,128)S(1)} fusion(f32[1536,128]{1,0:T(8,128)S(1)} %get-tuple-element.138, s32[3072]{0:T(1024)S(1)} %broadcast_clamp_fusion.2), kind=kCustom, calls=%fused_computation.clone.clone.1 | custom fusion | bytes 3158016 | tf_op jit(solution)/shard_map/while/body/eval_jaxpr/gather | solution.py:18
  270.0 2.0 copy.12
  272.0 74.0 %psum.22 = f32[128,16]{0,1:T(8,128)S(1)} all-reduce(f32[128,16]{0,1:T(8,128)S(1)} %fusion.5), channel_id=1, replica_groups=mesh['vgrp'=4,'samp'=64] {'vgrp','samp'}, use_global_device_ids=true, to_apply=%region_6.7 | all-reduce | flops 2048 | bytes 16384 | tf_op jit(solution)/shard_map/psum | solution.py:38
  347.8 11.7 %cholesky.16 = f32[128,128]{1,0:T(8,128)S(1)} custom-call(f32[128,128]{1,0:T(8,128)S(1)} %fusion.14), custom_call_target="Cholesky" | custom-call | tf_op jit(solution)/shard_map/jit(cholesky)/cholesky | solution.py:40
  360.9 9.8 %custom-call.8 = f32[1,128,128]{1,2,0:T(8,128)S(1)} custom-call(f32[1,128,128]{2,1,0:T(8,128)S(1)} %fusion.9), custom_call_target="InvertDiagBlocksLowerTriangular" | custom-call | tf_op jit(solution)/shard_map/triangular_solve | solution.py:9
  372.5 3.4 multiply_convert_fusion
  376.0 8.9 %convolution_bitcast_fusion = f32[512,2048]{0,1:T(8,128)} fusion(bf16[3072,2048]{0,1:T(8,128)(2,1)S(1)} %bitcast.45, s32[3072,512]{1,0:T(8,128)S(1)} %bitcast.51), kind=kOutput, calls=%fused_computation.19 | convolution fusion | flops 6444023808 | bytes 23068672 | tf_op jit(solution)/shard_map/dot_general | solution.py:52
  384.9 193.0 %all-reduce.5.cloned.1.call-done = f32[512,2048]{0,1:T(8,128)} async-done(((f32[512,2048]{0,1:T(8,128)}), f32[512,2048]{0,1:T(8,128)}) %all-reduce.5.cloned.1.call-update) | async-done | bytes 4194320 | tf_op jit(solution)/shard_map/psum | solution.py:52
  (102 shorter events, 48.9 us)
Async XLA Ops:
  6.5 339.5 %all-reduce.3.cloned.1.call-start = ((), (), s32[]{:S(2)}) async-start(), calls=%async_computation | async-start | bytes 131072 | tf_op jit(solution)/shard_map/psum | solution.py:38
  9.1 568.9 %all-reduce.5.cloned.1.call-start = ((), (), s32[]{:S(2)}) async-start(), calls=%async_computation.1 | async-start | bytes 8388608 | tf_op jit(solution)/shard_map/psum | solution.py:52
  270.0 101.1 %copy-start = (f32[3072,128]{1,0:T(8,128)S(1)}, f32[3072,128]{1,0:T(8,128)}, u32[]{:S(2)}) copy-start(f32[3072,128]{1,0:T(8,128)} %param.7) | copy-start | bytes 4718596
  371.1 4.9 slice-start
  372.5 3.5 slice-start.1
Sparse Core Ops, SparseCore 0:
  12.8 243.6 all-reduce.2
  385.1 192.8 all-reduce.4
where the time goes:
time: 588 us; the launch traced here: 587 us
  waiting for transfers between devices  193 us (33%)
  blocking collectives  151 us (26%)
  local copies, waits for them, and re-layouts  138 us (23%)
  other arithmetic  76.4 us (13%)
  matrix products  14.5 us (2%)
  between operations  13.5 us (2%)
    psum x1, waiting for transfers between devices, per_device(): lax.psum(jnp.dot(dosages.T, weighted, preferred_element_type=jnp.float32)...  193 us
    gather x16, local copies, waits for them, and re-layouts, one_perm(): picked_rows = table[index_row // 128]  130 us
    all_gather x1, blocking collectives, per_device(): pheno_full = lax.all_gather(phenotype, ('vgrp', 'samp'), axis=0, tiled=True)  77.2 us
    psum x1, blocking collectives, per_device(): gram, cross = lax.psum((gram_part, cross_part), ('vgrp', 'samp'))  74 us
    reduce_sum x16, other arithmetic, one_perm(): return jnp.sum(jnp.where(wanted, picked_rows, jnp.float32(0.0)), axis=1)  30.2 us
    select_n x16, other arithmetic, one_perm(): picked_rows = table[index_row // 128]  15.6 us
    another operation x3, other arithmetic, per_device(): factor = jnp.linalg.cholesky(system)  12.4 us
  transfers between devices with their start and end apart: 2, of which 1 were waited for; matrix products, arithmetic and copies ran while one was open for 31% of the time, Pallas kernels for 0%

commit v1 on v0

--- a/solution.py
+++ b/solution.py
@@ -24,7 +24,15 @@
 
 def per_device(phenotype, exposures, perms, genotypes):
     hi = lax.Precision.HIGHEST
-    pheno_full = lax.all_gather(phenotype, ("vgrp", "samp"), axis=0, tiled=True)
+    pheno_full = jnp.concatenate(
+        jax.lax.all_to_all(
+            jnp.stack(jax.lax.axis_size(("vgrp", "samp")) * [phenotype], axis=0),
+            axis_name=("vgrp", "samp"),
+            split_axis=0,
+            concat_axis=0,
+        ),
+        0,
+    )
     samples = pheno_full.shape[0]
     local_rows = exposures.shape[0]
     width = exposures.shape[1]

time: 588 us -> 772 us (1.31)
  waiting for transfers between devices: 193 us -> 438 us
  blocking collectives: 151 us -> 74.5 us
  starting transfers between devices: 0.04 us -> 14.7 us
    psum x1, waiting for transfers between devices: 0.01 us -> 246 us  [per_device(): gram, cross = lax.psum((gram_part, cross_part), ('vgrp', 'samp'))]
    all_gather x1 -> x0, blocking collectives: 77.2 us -> none  [per_device(): pheno_full = lax.all_gather(phenotype, ('vgrp', 'samp'), axis=0, tiled=True)]
    all_to_all x0 -> x1, starting transfers between devices: none -> 14.6 us  [per_device(): jax.lax.all_to_all(jnp.stack(jax.lax.axis_size(('vgrp', 'samp')) * [pheno...]
  transfers between devices with their start and end apart: 2 -> 3, of which waited for: 1 -> 2; matrix products, arithmetic and copies ran while one was open for 31% -> 4% of each run, Pallas kernels for 0% -> 0%
where the time goes in v1:
time: 772 us; the launch traced here: 771 us
  waiting for transfers between devices  438 us (57%)
  local copies, waits for them, and re-layouts  139 us (18%)
  other arithmetic  76.3 us (10%)
  blocking collectives  74.5 us (10%)
  matrix products  15.1 us (2%)
  starting transfers between devices  14.7 us (2%)
  between operations  13.6 us (2%)
    psum x1, waiting for transfers between devices, per_device(): gram, cross = lax.psum((gram_part, cross_part), ('vgrp', 'samp'))  246 us
    psum x1, waiting for transfers between devices, per_device(): lax.psum(jnp.dot(dosages.T, weighted, preferred_element_type=jnp.float32)...  192 us
    gather x16, local copies, waits for them, and re-layouts, one_perm(): picked_rows = table[index_row // 128]  130 us
    psum x1, blocking collectives, per_device(): gram, cross = lax.psum((gram_part, cross_part), ('vgrp', 'samp'))  74.5 us
    reduce_sum x16, other arithmetic, one_perm(): return jnp.sum(jnp.where(wanted, picked_rows, jnp.float32(0.0)), axis=1)  30.2 us
    select_n x16, other arithmetic, one_perm(): picked_rows = table[index_row // 128]  15.6 us
  transfers between devices with their start and end apart: 3, of which 2 were waited for; matrix products, arithmetic and copies ran while one was open for 4% of the time, Pallas kernels for 0%

profile of v1, /device:TPU:8, one launch (start us, length us, event | category | flops | bytes accessed | tf_op | source)
XLA Modules:
  0.0 771.4 jit_solution(2893386217389031496)
XLA Ops:
  6.5 2.1 stack.2
  8.6 14.6 %all-to-all-start = ((f32[256,1,768]{2,1,0:T(1,128)}), f32[256,1,768]{2,1,0:T(1,128)S(1)}, u32[]{:S(2)}, u32[]{:S(2)}) async-start(f32[256,1,768]{2,1,0:T(1,128)} %stack.2), calls=%async_computation | async-start | bytes 1572864 | tf_op jit(solution)/shard_map/all_to_all | solution.py:28
  26.5 245.7 %all-reduce.3.cloned.1.call-done = f32[128,128]{1,0:T(8,128)} async-done(((f32[128,128]{1,0:T(8,128)}), f32[128,128]{1,0:T(8,128)}) %all-reduce.3.cloned.1.call-update) | async-done | bytes 65552 | tf_op jit(solution)/shard_map/psum | solution.py:46
  274.0 11.7 %cholesky.16 = f32[128,128]{1,0:T(8,128)S(1)} custom-call(f32[128,128]{1,0:T(8,128)S(1)} %fusion.14), custom_call_target="Cholesky" | custom-call | tf_op jit(solution)/shard_map/jit(cholesky)/cholesky | solution.py:48
  286.9 9.8 %custom-call.8 = f32[1,128,128]{1,2,0:T(8,128)S(1)} custom-call(f32[1,128,128]{2,1,0:T(8,128)S(1)} %fusion.9), custom_call_target="InvertDiagBlocksLowerTriangular" | custom-call | tf_op jit(solution)/shard_map/triangular_solve | solution.py:9
  296.7 181.6 %while.13 = (s32[]{:T(128)}, f32[16,3072]{1,0:T(8,128)S(1)}, s32[16,3072]{1,0:T(8,128)}, f32[1536,128]{1,0:T(8,128)S(1)}, s32[]{:T(128)}, /*index=5*/s32[]{:T(128)}) while((s32[]{:T(128)}, f32[16,3072]{1,0:T(8,128)S(1)}, s32[16,3072]{1,0:T(8,128)}, f32[1536,128]{1,0:T(8,128)S(1)}, s32[]{:T(128)}, /*index=5*/s32[]{:T(128)}) %tuple.39), condition=%wide.region_2.3_spmd.clone, body=%wide.region_0.2_spmd.clone.sunk | while | flops 1268738 | bytes 4866133 | solution.py:22
  297.8 8.1 %gather_fusion = f32[3072,128]{1,0:T(8,128)S(1)} fusion(f32[1536,128]{1,0:T(8,128)S(1)} %get-tuple-element.138, s32[3072]{0:T(1024)S(1)} %broadcast_clamp_fusion.2), kind=kCustom, calls=%fused_computation.clone.clone.1 | custom fusion | bytes 3158016 | tf_op jit(solution)/shard_map/while/body/eval_jaxpr/gather | solution.py:18
  309.1 8.1 %gather_fusion = f32[3072,128]{1,0:T(8,128)S(1)} fusion(f32[1536,128]{1,0:T(8,128)S(1)} %get-tuple-element.138, s32[3072]{0:T(1024)S(1)} %broadcast_clamp_fusion.2), kind=kCustom, calls=%fused_computation.clone.clone.1 | custom fusion | bytes 3158016 | tf_op jit(solution)/shard_map/while/body/eval_jaxpr/gather | solution.py:18
  320.5 8.1 %gather_fusion = f32[3072,128]{1,0:T(8,128)S(1)} fusion(f32[1536,128]{1,0:T(8,128)S(1)} %get-tuple-element.138, s32[3072]{0:T(1024)S(1)} %broadcast_clamp_fusion.2), kind=kCustom, calls=%fused_computation.clone.clone.1 | custom fusion | bytes 3158016 | tf_op jit(solution)/shard_map/while/body/eval_jaxpr/gather | solution.py:18
  328.6 1.9 select_reduce_fusion.3
  331.8 8.1 %gather_fusion = f32[3072,128]{1,0:T(8,128)S(1)} fusion(f32[1536,128]{1,0:T(8,128)S(1)} %get-tuple-element.138, s32[3072]{0:T(1024)S(1)} %broadcast_clamp_fusion.2), kind=kCustom, calls=%fused_computation.clone.clone.1 | custom fusion | bytes 3158016 | tf_op jit(solution)/shard_map/while/body/eval_jaxpr/gather | solution.py:18
  339.9 1.9 select_reduce_fusion.3
  343.2 8.1 %gather_fusion = f32[3072,128]{1,0:T(8,128)S(1)} fusion(f32[1536,128]{1,0:T(8,128)S(1)} %get-tuple-element.138, s32[3072]{0:T(1024)S(1)} %broadcast_clamp_fusion.2), kind=kCustom, calls=%fused_computation.clone.clone.1 | custom fusion | bytes 3158016 | tf_op jit(solution)/shard_map/while/body/eval_jaxpr/gather | solution.py:18
  351.3 1.9 select_reduce_fusion.3
  354.5 8.1 %gather_fusion = f32[3072,128]{1,0:T(8,128)S(1)} fusion(f32[1536,128]{1,0:T(8,128)S(1)} %get-tuple-element.138, s32[3072]{0:T(1024)S(1)} %broadcast_clamp_fusion.2), kind=kCustom, calls=%fused_computation.clone.clone.1 | custom fusion | bytes 3158016 | tf_op jit(solution)/shard_map/while/body/eval_jaxpr/gather | solution.py:18
  365.9 8.1 %gather_fusion = f32[3072,128]{1,0:T(8,128)S(1)} fusion(f32[1536,128]{1,0:T(8,128)S(1)} %get-tuple-element.138, s32[3072]{0:T(1024)S(1)} %broadcast_clamp_fusion.2), kind=kCustom, calls=%fused_computation.clone.clone.1 | custom fusion | bytes 3158016 | tf_op jit(solution)/shard_map/while/body/eval_jaxpr/gather | solution.py:18
  377.2 8.1 %gather_fusion = f32[3072,128]{1,0:T(8,128)S(1)} fusion(f32[1536,128]{1,0:T(8,128)S(1)} %get-tuple-element.138, s32[3072]{0:T(1024)S(1)} %broadcast_clamp_fusion.2), kind=kCustom, calls=%fused_computation.clone.clone.1 | custom fusion | bytes 3158016 | tf_op jit(solution)/shard_map/while/body/eval_jaxpr/gather | solution.py:18
  385.4 1.9 select_reduce_fusion.3
  388.6 8.1 %gather_fusion = f32[3072,128]{1,0:T(8,128)S(1)} fusion(f32[1536,128]{1,0:T(8,128)S(1)} %get-tuple-element.138, s32[3072]{0:T(1024)S(1)} %broadcast_clamp_fusion.2), kind=kCustom, calls=%fused_computation.clone.clone.1 | custom fusion | bytes 3158016 | tf_op jit(solution)/shard_map/while/body/eval_jaxpr/gather | solution.py:18
  396.7 1.9 select_reduce_fusion.3
  399.9 8.1 %gather_fusion = f32[3072,128]{1,0:T(8,128)S(1)} fusion(f32[1536,128]{1,0:T(8,128)S(1)} %get-tuple-element.138, s32[3072]{0:T(1024)S(1)} %broadcast_clamp_fusion.2), kind=kCustom, calls=%fused_computation.clone.clone.1 | custom fusion | bytes 3158016 | tf_op jit(solution)/shard_map/while/body/eval_jaxpr/gather | solution.py:18
  411.3 8.1 %gather_fusion = f32[3072,128]{1,0:T(8,128)S(1)} fusion(f32[1536,128]{1,0:T(8,128)S(1)} %get-tuple-element.138, s32[3072]{0:T(1024)S(1)} %broadcast_clamp_fusion.2), kind=kCustom, calls=%fused_computation.clone.clone.1 | custom fusion | bytes 3158016 | tf_op jit(solution)/shard_map/while/body/eval_jaxpr/gather | solution.py:18
  422.6 8.1 %gather_fusion = f32[3072,128]{1,0:T(8,128)S(1)} fusion(f32[1536,128]{1,0:T(8,128)S(1)} %get-tuple-element.138, s32[3072]{0:T(1024)S(1)} %broadcast_clamp_fusion.2), kind=kCustom, calls=%fused_computation.clone.clone.1 | custom fusion | bytes 3158016 | tf_op jit(solution)/shard_map/while/body/eval_jaxpr/gather | solution.py:18
  434.0 8.1 %gather_fusion = f32[3072,128]{1,0:T(8,128)S(1)} fusion(f32[1536,128]{1,0:T(8,128)S(1)} %get-tuple-element.138, s32[3072]{0:T(1024)S(1)} %broadcast_clamp_fusion.2), kind=kCustom, calls=%fused_computation.clone.clone.1 | custom fusion | bytes 3158016 | tf_op jit(solution)/shard_map/while/body/eval_jaxpr/gather | solution.py:18
  445.3 8.1 %gather_fusion = f32[3072,128]{1,0:T(8,128)S(1)} fusion(f32[1536,128]{1,0:T(8,128)S(1)} %get-tuple-element.138, s32[3072]{0:T(1024)S(1)} %broadcast_clamp_fusion.2), kind=kCustom, calls=%fused_computation.clone.clone.1 | custom fusion | bytes 3158016 | tf_op jit(solution)/shard_map/while/body/eval_jaxpr/gather | solution.py:18
  456.7 8.1 %gather_fusion = f32[3072,128]{1,0:T(8,128)S(1)} fusion(f32[1536,128]{1,0:T(8,128)S(1)} %get-tuple-element.138, s32[3072]{0:T(1024)S(1)} %broadcast_clamp_fusion.2), kind=kCustom, calls=%fused_computation.clone.clone.1 | custom fusion | bytes 3158016 | tf_op jit(solution)/shard_map/while/body/eval_jaxpr/gather | solution.py:18
  468.0 8.1 %gather_fusion = f32[3072,128]{1,0:T(8,128)S(1)} fusion(f32[1536,128]{1,0:T(8,128)S(1)} %get-tuple-element.138, s32[3072]{0:T(1024)S(1)} %broadcast_clamp_fusion.2), kind=kCustom, calls=%fused_computation.clone.clone.1 | custom fusion | bytes 3158016 | tf_op jit(solution)/shard_map/while/body/eval_jaxpr/gather | solution.py:18
  479.8 74.5 %psum.22 = f32[128,16]{0,1:T(8,128)S(1)} all-reduce(f32[128,16]{0,1:T(8,128)S(1)} %fusion.5), channel_id=1, replica_groups=mesh['vgrp'=4,'samp'=64] {'vgrp','samp'}, use_global_device_ids=true, to_apply=%region_6.7 | all-reduce | flops 2048 | bytes 16384 | tf_op jit(solution)/shard_map/psum | solution.py:46
  554.6 3.0 fusion.3
  557.7 3.4 multiply_convert_fusion
  561.1 8.9 %convolution_bitcast_fusion = f32[512,2048]{0,1:T(8,128)} fusion(bf16[3072,2048]{0,1:T(8,128)(2,1)S(1)} %bitcast.45, s32[3072,512]{1,0:T(8,128)S(1)} %bitcast.51), kind=kOutput, calls=%fused_computation.19 | convolution fusion | flops 6444023808 | bytes 23068672 | tf_op jit(solution)/shard_map/dot_general | solution.py:60
  570.1 192.1 %all-reduce.5.cloned.1.call-done = f32[512,2048]{0,1:T(8,128)} async-done(((f32[512,2048]{0,1:T(8,128)}), f32[512,2048]{0,1:T(8,128)}) %all-reduce.5.cloned.1.call-update) | async-done | bytes 4194320 | tf_op jit(solution)/shard_map/psum | solution.py:60
  (105 shorter events, 51.8 us)
Async XLA Ops:
  6.5 16.8 %copy-start = (f32[3072,128]{1,0:T(8,128)S(1)}, f32[3072,128]{1,0:T(8,128)}, u32[]{:S(2)}) copy-start(f32[3072,128]{1,0:T(8,128)} %param.7) | copy-start | bytes 4718596
  8.6 288.1 %all-to-all-start = ((f32[256,1,768]{2,1,0:T(1,128)}), f32[256,1,768]{2,1,0:T(1,128)S(1)}, u32[]{:S(2)}, u32[]{:S(2)}) async-start(f32[256,1,768]{2,1,0:T(1,128)} %stack.2), calls=%async_computation | async-start | bytes 1572864 | tf_op jit(solution)/shard_map/all_to_all | solution.py:28
  23.3 248.9 %all-reduce.3.cloned.1.call-start = ((), (), s32[]{:S(2)}) async-start(), calls=%async_computation.1 | async-start | bytes 131072 | tf_op jit(solution)/shard_map/psum | solution.py:46
  24.8 737.4 %all-reduce.5.cloned.1.call-start = ((), (), s32[]{:S(2)}) async-start(), calls=%async_computation.2 | async-start | bytes 8388608 | tf_op jit(solution)/shard_map/psum | solution.py:60
  478.4 79.2 %copy-start.1 = (f32[3072,128]{0,1:T(8,128)S(1)}, f32[3072,128]{0,1:T(8,128)}, u32[]{:S(2)}) copy-start(f32[3072,128]{0,1:T(8,128)} %copy.12) | copy-start | bytes 4718596
  554.6 6.5 slice-start
  557.6 3.5 slice-start.1
Sparse Core Ops, SparseCore 0:
  29.6 242.5 all-reduce.2
  570.2 191.9 all-reduce.4
